TPU v7x, 512 devices: a whole 4x8x8 slice. The times are simulated.
512 devices in a mesh: dp: 16 (over z, core), expert: 32 (over x, y).
Axes of the slice: x: 4, y: 8, z: 8, core: 2. Of those that a mesh axis runs over, the one named last changes fastest.
Arguments:
- tokens: bfloat16 [65536, 1024], P(('dp', 'expert')), may hold values from -6 to 6
- expert_ids: int32 [65536, 8], P(('dp', 'expert')), may hold values from 0 to 63, all different within a row; in each aligned block of 128 rows (0 to 127, 128 to 255, ...) at most 17 rows name the same one
- gate_values: float32 [65536, 8], P(('dp', 'expert')), may hold values from 0.05 to 0.5
- w_gate: bfloat16 [64, 1024, 384], P('expert', 'dp'), may hold values from -0.1875 to 0.1875
- w_up: bfloat16 [64, 1024, 384], P('expert', 'dp'), may hold values from -0.1875 to 0.1875
- w_down: bfloat16 [64, 384, 1024], P('expert', 'dp'), may hold values from -0.3125 to 0.3125
- partner: int32 [512], replicated, may hold values from 0 to 511, as said below
Outputs:
- contrast_loss: float32 [], replicated
- token_grad: bfloat16 [65536, 1024], P(('dp', 'expert'))
- gate_grad: float32 [65536, 8], P(('dp', 'expert'))
Inputs may be any that keep to these rules, and one draw needn't show every extreme that they name: `expert_ids`: each row names 8 different experts. Among the 128 rows of one sequence no expert is named more than 17 times, and in every draw some sequence names some expert exactly 17 times. partner[i] differs from i.
All inputs are finite; a program needn't handle non-finite values.
Results may differ from a plain program's by a relative error of at most 0.014.
Values may be sent and summed in bfloat16 or wider, within the bound.
No kernel may reach another device: no remote copies, remote signals or barrier semaphores. Data moves between devices by JAX's collectives and lax.ppermute only.
A program may use at most 64 MiB of HBM per device.

v0:
```python
import jax
import jax.numpy as jnp
from jax import lax
from jax.sharding import PartitionSpec as P

score_scale = 20.0
highest = lax.Precision.HIGHEST


def silu_parts(pre_act):
    sigmoid_val = jax.nn.sigmoid(pre_act)
    return (pre_act * sigmoid_val, sigmoid_val * (1.0 + pre_act * (1.0 - sigmoid_val)))


def expert_forward(slot_piece, gate_full, up_full, down_full):
    pre_gate = jnp.einsum(
        "encd,edf->encf", slot_piece, gate_full, preferred_element_type=jnp.float32
    )
    pre_up = jnp.einsum("encd,edf->encf", slot_piece, up_full, preferred_element_type=jnp.float32)
    activated, derivative = silu_parts(pre_gate)
    hidden = (activated * pre_up).astype(jnp.bfloat16)
    expert_out = jnp.einsum(
        "encf,efd->encd", hidden, down_full, preferred_element_type=jnp.float32
    ).astype(jnp.bfloat16)
    return (expert_out, pre_gate, pre_up)


def on_device(tokens, expert_ids, gate_values, w_gate, w_up, w_down, partner):
    tok_rows, model_width = tokens.shape
    route_count = expert_ids.shape[1]
    local_experts = w_gate.shape[0]
    experts = lax.axis_size("expert") * local_experts
    capacity = tok_rows * route_count // experts + max(1, tok_rows * route_count // (16 * experts))
    slot_total = experts * capacity
    gate_full, up_full, down_full = (
        lax.all_gather(w_gate, "dp", axis=1, tiled=True),
        lax.all_gather(w_up, "dp", axis=1, tiled=True),
        lax.all_gather(w_down, "dp", axis=1, tiled=True),
    )
    expert_iota = jnp.arange(experts, dtype=jnp.int32)
    matches = expert_ids[:, :, None] == expert_iota
    chosen = jnp.sum(matches.astype(jnp.int32), axis=1, dtype=jnp.int32)
    chosen_gate = jnp.sum(jnp.where(matches, gate_values[:, :, None], 0.0), axis=1)
    before = jnp.cumsum(chosen, axis=0, dtype=jnp.int32) - chosen
    slot_rank = jnp.take_along_axis(before, expert_ids, axis=1)
    slot_row = (expert_ids * capacity + slot_rank).reshape(-1)
    slot_iota = jnp.arange(capacity, dtype=jnp.int32)
    onehot = (chosen.T[:, None, :] == 1) & (before.T[:, None, :] == slot_iota[None, :, None])
    placer = onehot.astype(jnp.bfloat16)
    slot_gate = jnp.sum(jnp.where(onehot, chosen_gate.T[:, None, :], 0.0), axis=2)
    outgoing = jnp.einsum("ect,td->ecd", placer, tokens, preferred_element_type=jnp.float32).astype(
        jnp.bfloat16
    )
    outgoing = outgoing.reshape(experts, 1, capacity, model_width)
    placer_flat = placer.reshape(slot_total, tok_rows)
    out_here, pre_gate, pre_up = expert_forward(
        lax.all_to_all(outgoing, "expert", split_axis=0, concat_axis=1, tiled=True),
        gate_full,
        up_full,
        down_full,
    )
    returned_out = lax.all_to_all(
        out_here, "expert", split_axis=1, concat_axis=0, tiled=True
    ).reshape(slot_total, model_width)
    weighted_sum = jnp.dot(
        slot_gate.reshape(slot_total), returned_out.astype(jnp.float32), precision=highest
    )
    pooled = jnp.mean(tokens.astype(jnp.float32), axis=0) + weighted_sum / tok_rows
    inv_rms = lax.rsqrt(jnp.mean(pooled * pooled) + 1e-06)
    embedding = (pooled * inv_rms).astype(jnp.bfloat16)[None, :]
    gathered = lax.all_gather(embedding, ("dp", "expert"), axis=0, tiled=True)
    batch_size = gathered.shape[0]
    own_index = lax.axis_index(("dp", "expert"))
    batch_iota = jnp.arange(batch_size, dtype=jnp.int32)
    scores = (
        score_scale
        / model_width
        * jnp.dot(gathered, embedding[0], preferred_element_type=jnp.float32)
    )
    others = batch_iota != own_index
    log_total = jnp.log(jnp.sum(jnp.where(others, jnp.exp(scores), 0.0)))
    own_partner = lax.dynamic_index_in_dim(partner, own_index, keepdims=False)
    partner_hit = (batch_iota == own_partner).astype(jnp.float32)
    weight = jnp.where(others, jnp.exp(scores - log_total), 0.0) - partner_hit
    all_embed = gathered.astype(jnp.float32)
    row_term = jnp.dot(weight, all_embed, precision=highest)
    all_totals = lax.all_gather(log_total[None], ("dp", "expert"), axis=0, tiled=True)
    column_weight = jnp.where(others, jnp.exp(scores - all_totals), 0.0) - (
        partner == own_index
    ).astype(jnp.float32)
    embed_grad = (
        score_scale
        / model_width
        * (row_term + jnp.dot(column_weight, all_embed, precision=highest))
    )
    partner_rows = jnp.take(gathered, partner, axis=0)
    partner_score = (
        score_scale
        / model_width
        * jnp.einsum("bd,bd->b", gathered, partner_rows, preferred_element_type=jnp.float32)
    )
    contrast_loss = jnp.mean(all_totals - partner_score)
    seq_grad = (
        inv_rms * embed_grad - inv_rms**3 * jnp.sum(pooled * embed_grad) / model_width * pooled
    )
    slot_dots = jnp.dot(returned_out.astype(jnp.float32), seq_grad, precision=highest)
    gate_grad = jnp.take(slot_dots, slot_row, axis=0).reshape(tok_rows, route_count)
    out_grad = (
        (slot_gate[:, :, None] * seq_grad)
        .astype(jnp.bfloat16)
        .reshape(experts, 1, capacity, model_width)
    )
    arrived = lax.all_to_all(out_grad, "expert", split_axis=0, concat_axis=1, tiled=True)
    hidden_grad = jnp.einsum(
        "encd,efd->encf", arrived, down_full, preferred_element_type=jnp.float32
    )
    activated, derivative = silu_parts(pre_gate)
    gate_side = (hidden_grad * pre_up * derivative).astype(jnp.bfloat16)
    up_side = (hidden_grad * activated).astype(jnp.bfloat16)
    route_here = jnp.einsum(
        "encf,edf->encd", gate_side, gate_full, preferred_element_type=jnp.float32
    )
    route_here = (
        route_here
        + jnp.einsum("encf,edf->encd", up_side, up_full, preferred_element_type=jnp.float32)
    ).astype(jnp.bfloat16)
    returned = lax.all_to_all(
        route_here, "expert", split_axis=1, concat_axis=0, tiled=True
    ).reshape(slot_total, model_width)
    route_sum = jnp.einsum("st,sd->td", placer_flat, returned, preferred_element_type=jnp.float32)
    token_grad = (seq_grad + route_sum).astype(jnp.bfloat16)
    return (contrast_loss, token_grad, gate_grad)


def solution(mesh):
    placed = (
        P(("dp", "expert"), None),
        P(("dp", "expert"), None),
        P(("dp", "expert"), None),
        P("expert", "dp", None),
        P("expert", "dp", None),
        P("expert", "dp", None),
        P(),
    )
    return jax.shard_map(
        on_device,
        mesh=mesh,
        in_specs=placed,
        out_specs=(P(), P(("dp", "expert"), None), P(("dp", "expert"), None)),
        check_vma=False,
    )
```

profile of v0, /device:TPU:16, one launch (start us, length us, event | category | flops | bytes accessed | tf_op | source)
XLA Modules:
  0.0 604.4 jit_solution(16274606224665401877)
XLA Ops:
  11.6 3.0 copy.118
  14.7 10.1 %all-to-all-start = ((bf16[64,1,17,1024]{3,2,1,0:T(8,128)(2,1)}), bf16[64,1,17,1024]{3,2,1,0:T(8,128)(2,1)S(1)}, u32[]{:S(2)}, u32[]{:S(2)}) async-start(bf16[64,1,17,1024]{3,2,1,0:T(8,128)(2,1)} %copy.118), calls=%async_computation | async-start | bytes 6291456 | tf_op jit(solution)/shard_map/all_to_all | solution.py:57
  25.5 31.7 %all-gather.6.cloned.1.call-done = bf16[2,1024,384]{2,1,0:T(8,128)(2,1)} async-done(((bf16[2,64,384]{2,1,0:T(8,128)(2,1)}), bf16[2,1024,384]{2,1,0:T(8,128)(2,1)}) %all-gather.6.cloned.1.call-update) | async-done | bytes 1572880 | tf_op jit(solution)/shard_map/all_gather | solution.py:36
  57.1 39.8 %all-to-all-done = bf16[64,1,17,1024]{3,2,1,0:T(8,128)(2,1)S(1)} async-done(((bf16[64,1,17,1024]{3,2,1,0:T(8,128)(2,1)}), bf16[64,1,17,1024]{3,2,1,0:T(8,128)(2,1)S(1)}, u32[]{:S(2)}, u32[]{:S(2)}) %all-to-all-start) | async-done | bytes 2228256 | tf_op jit(solution)/shard_map/all_to_all | solution.py:57
  96.9 4.3 fusion.5
  101.2 4.2 fusion.3
  105.4 37.3 %all-gather.10.cloned.1.call-done = bf16[2,384,1024]{2,1,0:T(8,128)(2,1)} async-done(((bf16[2,24,1024]{2,1,0:T(8,128)(2,1)}), bf16[2,384,1024]{2,1,0:T(8,128)(2,1)}) %all-gather.10.cloned.1.call-update) | async-done | bytes 1572880 | tf_op jit(solution)/shard_map/all_gather | solution.py:38
  142.7 3.8 convolution_convert_fusion
  146.5 3.7 copy.121
  150.2 10.0 %all-to-all-start.1 = ((bf16[2,32,17,1024]{3,0,2,1:T(2,128)(2,1)}), bf16[2,32,17,1024]{3,0,2,1:T(2,128)(2,1)S(1)}, u32[]{:S(2)}, u32[]{:S(2)}) async-start(bf16[2,32,17,1024]{3,0,2,1:T(2,128)(2,1)} %copy.121), calls=%async_computation.1 | async-start | bytes 4456448 | tf_op jit(solution)/shard_map/all_to_all | solution.py:62
  161.0 52.4 %all-to-all-done.1 = bf16[2,32,17,1024]{3,0,2,1:T(2,128)(2,1)S(1)} async-done(((bf16[2,32,17,1024]{3,0,2,1:T(2,128)(2,1)}), bf16[2,32,17,1024]{3,0,2,1:T(2,128)(2,1)S(1)}, u32[]{:S(2)}, u32[]{:S(2)}) %all-to-all-start.1) | async-done | bytes 2228256 | tf_op jit(solution)/shard_map/all_to_all | solution.py:62
  213.4 2.7 copy.122
  216.1 3.0 reshape.128
  225.1 102.9 %all-gather.12.cloned.1.call-done = bf16[524288]{0:T(1024)(128)(2,1)} async-done(((bf16[1024]{0:T(1024)(128)(2,1)}), bf16[524288]{0:T(1024)(128)(2,1)}) %all-gather.12.cloned.1.call-update) | async-done | bytes 1048592 | tf_op jit(solution)/shard_map/all_gather | solution.py:71
  333.8 97.6 %all-reduce = f32[512]{0:T(512)} all-reduce(f32[512]{0:T(512)} %dynamic-update-slice), channel_id=1, replica_groups=mesh['dp'=16,'expert'=32] {'dp','expert'}, use_global_device_ids=true, to_apply=%add | all-reduce | flops 512 | bytes 4096
  431.4 2.9 gather_fusion
  441.6 79.0 %all_to_all.66 = bf16[64,1,17,1024]{3,2,1,0:T(8,128)(2,1)S(1)} all-to-all(bf16[64,1,17,1024]{3,2,1,0:T(8,128)(2,1)S(1)} %multiply_convert_fusion), channel_id=1, replica_groups=mesh['dp'=16,'expert'=32] {'expert'}, dimensions={0} | all-to-all | bytes 4456448 | tf_op jit(solution)/shard_map/all_to_all | solution.py:113
  526.0 3.7 copy.125
  529.6 6.9 %all-to-all-start.3 = ((bf16[2,32,17,1024]{3,0,2,1:T(2,128)(2,1)}), bf16[2,32,17,1024]{3,0,2,1:T(2,128)(2,1)}, u32[]{:S(2)}, u32[]{:S(2)}) async-start(bf16[2,32,17,1024]{3,0,2,1:T(2,128)(2,1)} %copy.125), calls=%async_computation.3 | async-start | bytes 4456448 | tf_op jit(solution)/shard_map/all_to_all | solution.py:127
  537.6 7.1 %gather_fusion.2 = s32[1024]{0:T(1024)S(1)} fusion(s32[128,64]{1,0:T(8,128)S(1)} %sub.31, s32[1024]{0:T(1024)S(1)} %reshape.148), kind=kCustom, calls=%fused_computation.2 | custom fusion | bytes 16384 | tf_op jit(solution)/shard_map/jit(take_along_axis)/gather | solution.py:45
  546.9 6.2 %gather_fusion.1 = f32[1024]{0:T(1024)S(1)} fusion(f32[1088]{0:T(1024)S(1)} %convolution_reduce_fusion, s32[1024]{0:T(1024)S(1)} %broadcast_clamp_fusion), kind=kCustom, calls=%fused_computation.1 | custom fusion | bytes 12288 | tf_op jit(solution)/shard_map/jit(_take)/gather | solution.py:107
  554.5 34.5 %all-to-all-done.3 = bf16[2,32,17,1024]{3,0,2,1:T(2,128)(2,1)} async-done(((bf16[2,32,17,1024]{3,0,2,1:T(2,128)(2,1)}), bf16[2,32,17,1024]{3,0,2,1:T(2,128)(2,1)}, u32[]{:S(2)}, u32[]{:S(2)}) %all-to-all-start.3) | async-done | bytes 2228256 | tf_op jit(solution)/shard_map/all_to_all | solution.py:127
  589.0 2.5 copy.126
  593.8 2.9 fusion.18
  (86 shorter events, 34.4 us)
Async XLA Ops:
  7.2 50.0 %all-gather.6.cloned.1.call-start = ((), (), s32[]{:S(2)}) async-start(), calls=%async_computation.4 | async-start | bytes 1671168 | tf_op jit(solution)/shard_map/all_gather | solution.py:36
  7.9 93.3 %all-gather.8.cloned.1.call-start = ((), (), s32[]{:S(2)}) async-start(), calls=%async_computation.5 | async-start | bytes 1671168 | tf_op jit(solution)/shard_map/all_gather | solution.py:37
  14.7 82.3 %all-to-all-start = ((bf16[64,1,17,1024]{3,2,1,0:T(8,128)(2,1)}), bf16[64,1,17,1024]{3,2,1,0:T(8,128)(2,1)S(1)}, u32[]{:S(2)}, u32[]{:S(2)}) async-start(bf16[64,1,17,1024]{3,2,1,0:T(8,128)(2,1)} %copy.118), calls=%async_computation | async-start | bytes 6291456 | tf_op jit(solution)/shard_map/all_to_all | solution.py:57
  24.7 118.0 %all-gather.10.cloned.1.call-start = ((), (), s32[]{:S(2)}) async-start(), calls=%async_computation.6 | async-start | bytes 1671168 | tf_op jit(solution)/shard_map/all_gather | solution.py:38
  150.2 10.2 %copy-start.3 = (s32[128,8]{0,1:T(8,128)S(1)}, s32[128,8]{0,1:T(8,128)}, u32[]{:S(2)}) copy-start(s32[128,8]{0,1:T(8,128)} %param.8) | copy-start | bytes 12292
  150.2 10.2 %copy-start.7 = (f32[128,8]{0,1:T(8,128)S(1)}, f32[128,8]{0,1:T(8,128)}, u32[]{:S(2)}) copy-start(f32[128,8]{0,1:T(8,128)} %param.9) | copy-start | bytes 12292
  150.2 10.7 %copy-start = (bf16[128,1024]{1,0:T(8,128)(2,1)S(1)}, bf16[128,1024]{1,0:T(8,128)(2,1)}, u32[]{:S(2)}) copy-start(bf16[128,1024]{1,0:T(8,128)(2,1)} %param.7) | copy-start | bytes 786436
  150.2 63.2 %all-to-all-start.1 = ((bf16[2,32,17,1024]{3,0,2,1:T(2,128)(2,1)}), bf16[2,32,17,1024]{3,0,2,1:T(2,128)(2,1)S(1)}, u32[]{:S(2)}, u32[]{:S(2)}) async-start(bf16[2,32,17,1024]{3,0,2,1:T(2,128)(2,1)} %copy.121), calls=%async_computation.1 | async-start | bytes 4456448 | tf_op jit(solution)/shard_map/all_to_all | solution.py:62
  160.2 167.7 %all-gather.12.cloned.1.call-start = ((), (), s32[]{:S(2)}) async-start(), calls=%async_computation.7 | async-start | bytes 1050624 | tf_op jit(solution)/shard_map/all_gather | solution.py:71
  160.8 55.3 %copy-start.2 = (f32[64,17]{1,0:T(8,128)}, f32[64,17]{1,0:T(8,128)S(1)}, u32[]{:S(2)}) copy-start(f32[64,17]{1,0:T(8,128)S(1)} %select_reduce_fusion) | copy-start | bytes 13060
  219.1 2.9 copy-start.5
  434.3 1.8 copy-start.6
  438.4 1.3 copy-start.4
  441.6 79.0 %copy-start.10 = (bf16[2,384,1024]{2,1,0:T(8,128)(2,1)S(1)}, bf16[2,384,1024]{2,1,0:T(8,128)(2,1)}, u32[]{:S(2)}) copy-start(bf16[2,384,1024]{2,1,0:T(8,128)(2,1)} %all-gather.10.cloned.1.call-done) | copy-start | bytes 4718596
  520.6 1.8 copy-start.8
  520.6 1.9 copy-start.11
  520.6 2.4 copy-start.12
  523.0 1.5 copy-start.9
  529.6 59.3 %all-to-all-start.3 = ((bf16[2,32,17,1024]{3,0,2,1:T(2,128)(2,1)}), bf16[2,32,17,1024]{3,0,2,1:T(2,128)(2,1)}, u32[]{:S(2)}, u32[]{:S(2)}) async-start(bf16[2,32,17,1024]{3,0,2,1:T(2,128)(2,1)} %copy.125), calls=%async_computation.3 | async-start | bytes 4456448 | tf_op jit(solution)/shard_map/all_to_all | solution.py:127
  591.5 2.3 copy-start.1
Sparse Core Ops, SparseCore 0:
  10.1 46.9 all-gather.5
  59.3 40.5 all-gather.7
  102.1 40.6 all-gather.9
  222.1 105.7 all-gather.11
where the time goes:
time: 605 us; the launch traced here: 604 us
  waiting for transfers between devices  301 us (50%)
  blocking collectives  177 us (29%)
  local copies, waits for them, and re-layouts  44.9 us (7%)
  starting transfers between devices  27.3 us (5%)
  matrix products  26.4 us (4%)
  between operations  18 us (3%)
  other arithmetic  10.6 us (2%)
    all_gather x1, waiting for transfers between devices, on_device(): gathered = lax.all_gather(embedding, ('dp', 'expert'), axis=0, tiled=True)  103 us
    unnamed x1, blocking collectives  97.6 us
    all_to_all x1, blocking collectives, on_device(): lax.all_to_all(out_grad, 'expert', split_axis=0, concat_axis=1, tiled=True)  79 us
    all_to_all x1, waiting for transfers between devices, on_device(): lax.all_to_all(out_here, 'expert', split_axis=1, concat_axis=0, tiled=True)  52.4 us
    all_to_all x1, waiting for transfers between devices, on_device(): lax.all_to_all(outgoing, 'expert', split_axis=0, concat_axis=1, tiled=True)  39.8 us
    all_gather x1, waiting for transfers between devices, on_device(): lax.all_gather(w_down, 'dp', axis=1, tiled=True)  37.3 us
    all_to_all x1, waiting for transfers between devices, on_device(): lax.all_to_all(route_here, 'expert', split_axis=1, concat_axis=0, tiled=T...  34.5 us
    all_gather x1, waiting for transfers between devices, on_device(): lax.all_gather(w_gate, 'dp', axis=1, tiled=True)  31.7 us
  transfers between devices with their start and end apart: 7, of which 6 were waited for; matrix products, arithmetic and copies ran while one was open for 6% of the time, Pallas kernels for 0%

commit v1 on v0

--- a/solution.py
+++ b/solution.py
@@ -26,6 +26,13 @@
 
 
 def on_device(tokens, expert_ids, gate_values, w_gate, w_up, w_down, partner):
+
+    def supply_all_the_slot(body, ax_name, where_dim):
+        arr_out = tuple((body for _ in range(lax.axis_size(ax_name))))
+        after = jnp.stack(arr_out, axis=0)
+        piece_out = lax.all_to_all(after, split_axis=0, axis_name=ax_name, concat_axis=0)
+        return jnp.concatenate(piece_out, axis=where_dim)
+
     tok_rows, model_width = tokens.shape
     route_count = expert_ids.shape[1]
     local_experts = w_gate.shape[0]
@@ -68,7 +75,7 @@
     pooled = jnp.mean(tokens.astype(jnp.float32), axis=0) + weighted_sum / tok_rows
     inv_rms = lax.rsqrt(jnp.mean(pooled * pooled) + 1e-06)
     embedding = (pooled * inv_rms).astype(jnp.bfloat16)[None, :]
-    gathered = lax.all_gather(embedding, ("dp", "expert"), axis=0, tiled=True)
+    gathered = supply_all_the_slot(embedding, ax_name=("dp", "expert"), where_dim=0)
     batch_size = gathered.shape[0]
     own_index = lax.axis_index(("dp", "expert"))
     batch_iota = jnp.arange(batch_size, dtype=jnp.int32)

time: 605 us -> 564 us (0.932); the launches traced: 604 us -> 556 us
  waiting for transfers between devices: 301 us -> 228 us
  starting transfers between devices: 27.3 us -> 38.9 us
  other arithmetic: 10.6 us -> 18.8 us
  local copies, waits for them, and re-layouts: 44.9 us -> 52.3 us
    all_gather x1 -> x0, waiting for transfers between devices: 103 us -> none  [on_device(): gathered = lax.all_gather(embedding, ('dp', 'expert'), axis=0, tiled=True)]
    all_to_all x0 -> x1, waiting for transfers between devices: none -> 29.9 us  [supply_all_the_slot(): lax.all_to_all(after, split_axis=0, axis_name=ax_name, concat_axis=0)]
    all_to_all x0 -> x1, starting transfers between devices: none -> 11.2 us  [supply_all_the_slot(): lax.all_to_all(after, split_axis=0, axis_name=ax_name, concat_axis=0)]
    another operation x0 -> x1, other arithmetic: none -> 8.03 us  [supply_all_the_slot(): after = jnp.stack(arr_out, axis=0)]
    unnamed x28 -> x33, local copies, waits for them, and re-layouts: 2.64 us -> 9.58 us
where the time goes in v1:
time: 564 us; the launch traced here: 556 us
  waiting for transfers between devices  228 us (40%)
  blocking collectives  174 us (31%)
  local copies, waits for them, and re-layouts  52.3 us (9%)
  starting transfers between devices  38.9 us (7%)
  matrix products  25.7 us (5%)
  other arithmetic  18.8 us (3%)
  between operations  18.1 us (3%)
    unnamed x1, blocking collectives  93.5 us
    all_to_all x1, blocking collectives, on_device(): lax.all_to_all(out_grad, 'expert', split_axis=0, concat_axis=1, tiled=True)  80.4 us
    all_to_all x1, waiting for transfers between devices, on_device(): lax.all_to_all(out_here, 'expert', split_axis=1, concat_axis=0, tiled=True)  52.5 us
    all_to_all x1, waiting for transfers between devices, on_device(): lax.all_to_all(outgoing, 'expert', split_axis=0, concat_axis=1, tiled=True)  39.7 us
    all_gather x1, waiting for transfers between devices, on_device(): lax.all_gather(w_down, 'dp', axis=1, tiled=True)  37.4 us
    all_to_all x1, waiting for transfers between devices, on_device(): lax.all_to_all(route_here, 'expert', split_axis=1, concat_axis=0, tiled=T...  34.6 us
    all_gather x1, waiting for transfers between devices, on_device(): lax.all_gather(w_gate, 'dp', axis=1, tiled=True)  31.7 us
    all_to_all x1, waiting for transfers between devices, supply_all_the_slot(): lax.all_to_all(after, split_axis=0, axis_name=ax_name, concat_axis=0)  29.9 us
  transfers between devices with their start and end apart: 7, of which 6 were waited for; matrix products, arithmetic and copies ran while one was open for 6% of the time, Pallas kernels for 0%

profile of v1, /device:TPU:16, one launch (start us, length us, event | category | flops | bytes accessed | tf_op | source)
XLA Modules:
  0.0 555.5 jit_solution(12222734986261897400)
XLA Ops:
  11.6 3.0 copy.118
  14.6 10.1 %all-to-all-start = ((bf16[64,1,17,1024]{3,2,1,0:T(8,128)(2,1)}), bf16[64,1,17,1024]{3,2,1,0:T(8,128)(2,1)S(1)}, u32[]{:S(2)}, u32[]{:S(2)}) async-start(bf16[64,1,17,1024]{3,2,1,0:T(8,128)(2,1)} %copy.118), calls=%async_computation | async-start | bytes 6291456 | tf_op jit(solution)/shard_map/all_to_all | solution.py:64
  25.4 31.7 %all-gather.4.cloned.1.call-done = bf16[2,1024,384]{2,1,0:T(8,128)(2,1)} async-done(((bf16[2,64,384]{2,1,0:T(8,128)(2,1)}), bf16[2,1024,384]{2,1,0:T(8,128)(2,1)}) %all-gather.4.cloned.1.call-update) | async-done | bytes 1572880 | tf_op jit(solution)/shard_map/all_gather | solution.py:43
  57.1 39.7 %all-to-all-done = bf16[64,1,17,1024]{3,2,1,0:T(8,128)(2,1)S(1)} async-done(((bf16[64,1,17,1024]{3,2,1,0:T(8,128)(2,1)}), bf16[64,1,17,1024]{3,2,1,0:T(8,128)(2,1)S(1)}, u32[]{:S(2)}, u32[]{:S(2)}) %all-to-all-start) | async-done | bytes 2228256 | tf_op jit(solution)/shard_map/all_to_all | solution.py:64
  96.9 4.2 fusion.5
  101.1 4.2 fusion.3
  105.4 37.4 %all-gather.8.cloned.1.call-done = bf16[2,384,1024]{2,1,0:T(8,128)(2,1)} async-done(((bf16[2,24,1024]{2,1,0:T(8,128)(2,1)}), bf16[2,384,1024]{2,1,0:T(8,128)(2,1)}) %all-gather.8.cloned.1.call-update) | async-done | bytes 1572880 | tf_op jit(solution)/shard_map/all_gather | solution.py:45
  142.7 3.8 convolution_convert_fusion
  146.5 3.7 copy.121
  150.2 10.5 %all-to-all-start.1 = ((bf16[2,32,17,1024]{3,0,2,1:T(2,128)(2,1)}), bf16[2,32,17,1024]{3,0,2,1:T(2,128)(2,1)S(1)}, u32[]{:S(2)}, u32[]{:S(2)}) async-start(bf16[2,32,17,1024]{3,0,2,1:T(2,128)(2,1)} %copy.121), calls=%async_computation.1 | async-start | bytes 4456448 | tf_op jit(solution)/shard_map/all_to_all | solution.py:69
  161.3 52.5 %all-to-all-done.1 = bf16[2,32,17,1024]{3,0,2,1:T(2,128)(2,1)S(1)} async-done(((bf16[2,32,17,1024]{3,0,2,1:T(2,128)(2,1)}), bf16[2,32,17,1024]{3,0,2,1:T(2,128)(2,1)S(1)}, u32[]{:S(2)}, u32[]{:S(2)}) %all-to-all-start.1) | async-done | bytes 2228256 | tf_op jit(solution)/shard_map/all_to_all | solution.py:69
  216.4 3.0 reshape.133
  224.7 8.0 %reduce.4 = bf16[512,1024]{1,0:T(8,128)(2,1)S(1)} reduce(bf16[512,1,1024]{2,1,0:T(2,128)(2,1)} %stack.3, bf16[]{:T(256)} %broadcast.162), dimensions={1}, to_apply=%stack.3.reduce_sub_computation | reduce | bytes 2097154 | tf_op jit(solution)/shard_map/stack | solution.py:32
  234.3 11.2 %all-to-all-start.2 = ((bf16[512,2,512]{2,1,0:T(2,128)(2,1)}), bf16[512,2,512]{2,1,0:T(2,128)(2,1)S(1)}, u32[]{:S(2)}, u32[]{:S(2)}) async-start(bf16[512,2,512]{2,1,0:T(2,128)(2,1)} %reshape.187), calls=%async_computation.2 | async-start | bytes 2097152 | tf_op jit(solution)/shard_map/all_to_all | solution.py:33
  247.9 29.9 %all-to-all-done.2 = bf16[512,2,512]{2,1,0:T(2,128)(2,1)S(1)} async-done(((bf16[512,2,512]{2,1,0:T(2,128)(2,1)}), bf16[512,2,512]{2,1,0:T(2,128)(2,1)S(1)}, u32[]{:S(2)}, u32[]{:S(2)}) %all-to-all-start.2) | async-done | bytes 1048608 | tf_op jit(solution)/shard_map/all_to_all | solution.py:33
  277.8 3.3 reshape.188
  286.7 93.5 %all-reduce = f32[512]{0:T(512)} all-reduce(f32[512]{0:T(512)} %dynamic-update-slice), channel_id=1, replica_groups=mesh['dp'=16,'expert'=32] {'dp','expert'}, use_global_device_ids=true, to_apply=%add | all-reduce | flops 512 | bytes 4096
  380.3 2.9 gather_fusion
  391.1 80.4 %all_to_all.71 = bf16[64,1,17,1024]{3,2,1,0:T(8,128)(2,1)S(1)} all-to-all(bf16[64,1,17,1024]{3,2,1,0:T(8,128)(2,1)S(1)} %multiply_convert_fusion), channel_id=1, replica_groups=mesh['dp'=16,'expert'=32] {'expert'}, dimensions={0} | all-to-all | bytes 4456448 | tf_op jit(solution)/shard_map/all_to_all | solution.py:120
  476.9 3.7 copy.125
  480.6 7.0 %all-to-all-start.4 = ((bf16[2,32,17,1024]{3,0,2,1:T(2,128)(2,1)}), bf16[2,32,17,1024]{3,0,2,1:T(2,128)(2,1)}, u32[]{:S(2)}, u32[]{:S(2)}) async-start(bf16[2,32,17,1024]{3,0,2,1:T(2,128)(2,1)} %copy.125), calls=%async_computation.4 | async-start | bytes 4456448 | tf_op jit(solution)/shard_map/all_to_all | solution.py:134
  488.5 7.1 %gather_fusion.2 = s32[1024]{0:T(1024)S(1)} fusion(s32[128,64]{1,0:T(8,128)S(1)} %sub.31, s32[1024]{0:T(1024)S(1)} %reshape.154), kind=kCustom, calls=%fused_computation.2 | custom fusion | bytes 16384 | tf_op jit(solution)/shard_map/jit(take_along_axis)/gather | solution.py:52
  497.8 6.2 %gather_fusion.1 = f32[1024]{0:T(1024)S(1)} fusion(f32[1088]{0:T(1024)S(1)} %convolution_reduce_fusion, s32[1024]{0:T(1024)S(1)} %broadcast_clamp_fusion), kind=kCustom, calls=%fused_computation.1 | custom fusion | bytes 12288 | tf_op jit(solution)/shard_map/jit(_take)/gather | solution.py:114
  505.3 34.6 %all-to-all-done.4 = bf16[2,32,17,1024]{3,0,2,1:T(2,128)(2,1)} async-done(((bf16[2,32,17,1024]{3,0,2,1:T(2,128)(2,1)}), bf16[2,32,17,1024]{3,0,2,1:T(2,128)(2,1)}, u32[]{:S(2)}, u32[]{:S(2)}) %all-to-all-start.4) | async-done | bytes 2228256 | tf_op jit(solution)/shard_map/all_to_all | solution.py:134
  (92 shorter events, 45.9 us)
Async XLA Ops:
  7.2 50.0 %all-gather.4.cloned.1.call-start = ((), (), s32[]{:S(2)}) async-start(), calls=%async_computation.5 | async-start | bytes 1671168 | tf_op jit(solution)/shard_map/all_gather | solution.py:43
  7.9 93.2 %all-gather.6.cloned.1.call-start = ((), (), s32[]{:S(2)}) async-start(), calls=%async_computation.6 | async-start | bytes 1671168 | tf_op jit(solution)/shard_map/all_gather | solution.py:44
  14.6 82.3 %all-to-all-start = ((bf16[64,1,17,1024]{3,2,1,0:T(8,128)(2,1)}), bf16[64,1,17,1024]{3,2,1,0:T(8,128)(2,1)S(1)}, u32[]{:S(2)}, u32[]{:S(2)}) async-start(bf16[64,1,17,1024]{3,2,1,0:T(8,128)(2,1)} %copy.118), calls=%async_computation | async-start | bytes 6291456 | tf_op jit(solution)/shard_map/all_to_all | solution.py:64
  24.7 118.0 %all-gather.8.cloned.1.call-start = ((), (), s32[]{:S(2)}) async-start(), calls=%async_computation.7 | async-start | bytes 1671168 | tf_op jit(solution)/shard_map/all_gather | solution.py:45
  150.2 10.5 %copy-start.3 = (s32[128,8]{0,1:T(8,128)S(1)}, s32[128,8]{0,1:T(8,128)}, u32[]{:S(2)}) copy-start(s32[128,8]{0,1:T(8,128)} %param.8) | copy-start | bytes 12292
  150.2 10.6 %copy-start.8 = (f32[128,8]{0,1:T(8,128)S(1)}, f32[128,8]{0,1:T(8,128)}, u32[]{:S(2)}) copy-start(f32[128,8]{0,1:T(8,128)} %param.9) | copy-start | bytes 12292
  150.2 11.1 %copy-start = (bf16[128,1024]{1,0:T(8,128)(2,1)S(1)}, bf16[128,1024]{1,0:T(8,128)(2,1)}, u32[]{:S(2)}) copy-start(bf16[128,1024]{1,0:T(8,128)(2,1)} %param.7) | copy-start | bytes 786436
  150.2 63.6 %all-to-all-start.1 = ((bf16[2,32,17,1024]{3,0,2,1:T(2,128)(2,1)}), bf16[2,32,17,1024]{3,0,2,1:T(2,128)(2,1)S(1)}, u32[]{:S(2)}, u32[]{:S(2)}) async-start(bf16[2,32,17,1024]{3,0,2,1:T(2,128)(2,1)} %copy.121), calls=%async_computation.1 | async-start | bytes 4456448 | tf_op jit(solution)/shard_map/all_to_all | solution.py:69
  161.1 55.3 %copy-start.2 = (f32[64,17]{1,0:T(8,128)}, f32[64,17]{1,0:T(8,128)S(1)}, u32[]{:S(2)}) copy-start(f32[64,17]{1,0:T(8,128)S(1)} %select_reduce_fusion) | copy-start | bytes 13060
  232.7 12.8 %copy-start.5 = (s32[512]{0:T(512)S(1)}, s32[512]{0:T(512)}, u32[]{:S(2)}) copy-start(s32[512]{0:T(512)} %param.13) | copy-start | bytes 6148
  234.3 43.5 %all-to-all-start.2 = ((bf16[512,2,512]{2,1,0:T(2,128)(2,1)}), bf16[512,2,512]{2,1,0:T(2,128)(2,1)S(1)}, u32[]{:S(2)}, u32[]{:S(2)}) async-start(bf16[512,2,512]{2,1,0:T(2,128)(2,1)} %reshape.187), calls=%async_computation.2 | async-start | bytes 2097152 | tf_op jit(solution)/shard_map/all_to_all | solution.py:33
  281.1 2.0 copy-start.6
  383.2 2.5 copy-start.7
  388.0 1.3 copy-start.4
  391.1 80.4 %copy-start.11 = (bf16[2,384,1024]{2,1,0:T(8,128)(2,1)S(1)}, bf16[2,384,1024]{2,1,0:T(8,128)(2,1)}, u32[]{:S(2)}) copy-start(bf16[2,384,1024]{2,1,0:T(8,128)(2,1)} %all-gather.8.cloned.1.call-done) | copy-start | bytes 4718596
  471.5 1.8 copy-start.9
  471.5 1.9 copy-start.12
  471.5 2.4 copy-start.13
  474.0 1.5 copy-start.10
  480.6 59.4 %all-to-all-start.4 = ((bf16[2,32,17,1024]{3,0,2,1:T(2,128)(2,1)}), bf16[2,32,17,1024]{3,0,2,1:T(2,128)(2,1)}, u32[]{:S(2)}, u32[]{:S(2)}) async-start(bf16[2,32,17,1024]{3,0,2,1:T(2,128)(2,1)} %copy.125), calls=%async_computation.4 | async-start | bytes 4456448 | tf_op jit(solution)/shard_map/all_to_all | solution.py:134
  542.5 2.3 copy-start.1
Sparse Core Ops, SparseCore 0:
  10.1 46.9 all-gather.3
  59.3 40.5 all-gather.5
  102.1 40.6 all-gather.7
